TPU v7x, 256 devices: a whole 4x4x8 slice. The times are simulated.
256 devices in a mesh: clip: 4 (over z_hi, core), fsdp: 64 (over y, z_lo, x).
Axes of the slice: x: 4, y: 4, z: 8 (z_hi: 2, z_lo: 4; z = z_hi * 4 + z_lo), core: 2. Of those that a mesh axis runs over, the one named last changes fastest.
Arguments:
- span_queries: bfloat16 [64, 512, 2560], P('fsdp', None, 'clip'), may hold values from -20 to 20
- span_keys: bfloat16 [64, 512, 2560], P('fsdp', None, 'clip'), may hold values from -12 to 12
- span_values: bfloat16 [64, 512, 2560], P('fsdp', None, 'clip'), may hold values from -6 to 6
- cache_keys: bfloat16 [128, 512, 2560], P(None, 'fsdp', 'clip'), may hold values from -6 to 6
- cache_values: bfloat16 [128, 512, 2560], P(None, 'fsdp', 'clip'), may hold values from -6 to 6
- page_table: int32 [128], replicated, may hold values from 0 to 127, each once
- frame_lists: int32 [64, 6], replicated, may hold values from 0 to 15, as said below
- list_counts: int32 [64], replicated, may hold values from 1 to 6, as said below
- out_weight: bfloat16 [2560, 5120], P('clip', 'fsdp'), may hold values from -1 to 1
Outputs:
- projected: bfloat16 [64, 512, 5120], P('fsdp', 'clip')
Inputs may be any that keep to these rules, and one draw needn't show every extreme that they name: `frame_lists`: each row holds 6 different cached frames; a frame attends to the first list_counts of them. `list_counts`: the counts of frames 2 * i and 2 * i + 1 sum to exactly 7; some frame attends to exactly 6. `page_table`: every block number once.
All inputs are finite; a program needn't handle non-finite values.
Results may differ from a plain program's by a relative error of at most 0.017.
Values may be sent and summed in bfloat16 or wider, within the bound.
No kernel may reach another device: no remote copies, remote signals or barrier semaphores. Data moves between devices by JAX's collectives and lax.ppermute only.
A program may use at most 128 MiB of HBM per device.

v0:
```python
import math
import jax
import jax.numpy as jnp
import numpy as np
from jax import lax
from jax.sharding import Mesh
from jax.sharding import PartitionSpec as P

HD = 128
CF = 8
NC = 16
FRAME_AXES = ("y", "zl", "x")
neg_fill = -1e30


def empty_state(tokens_here, heads_here):
    return (
        jnp.full((tokens_here, heads_here), neg_fill, jnp.float32),
        jnp.zeros((tokens_here, heads_here), jnp.float32),
        jnp.zeros((tokens_here, heads_here, HD), jnp.float32),
    )


def absorb(carried, query_block, key_block, value_block):
    running_max, running_sum, running_out = carried
    scores = jnp.einsum(
        "qhd,khd->qhk", query_block, key_block, preferred_element_type=jnp.float32
    ) * (1.0 / math.sqrt(HD))
    new_max = jnp.maximum(running_max, jnp.max(scores, axis=2))
    shrink = jnp.exp(running_max - new_max)
    weights = jnp.exp(scores - new_max[:, :, None])
    running_sum = running_sum * shrink + jnp.sum(weights, axis=2)
    running_out = running_out * shrink[:, :, None] + jnp.einsum(
        "qhk,khd->qhd",
        weights.astype(jnp.bfloat16),
        value_block,
        preferred_element_type=jnp.float32,
    )
    return (new_max, running_sum, running_out)


def pair_schedule(frames, half_slots, page_table, frame_lists, list_counts):
    dest = jnp.arange(frames, dtype=jnp.int32)[:, None]
    slot = jnp.arange(half_slots, dtype=jnp.int32)[None, :]
    even = dest - dest % 2
    global_half = dest % 2 * half_slots + slot
    combined = global_half // 2
    row_half = global_half % 2
    even_count = list_counts[even]
    for_even = combined < even_count
    listed_even = frame_lists[even, jnp.minimum(combined, frame_lists.shape[1] - 1)]
    listed_odd = frame_lists[even + 1, jnp.clip(combined - even_count, 0, frame_lists.shape[1] - 1)]
    listed = jnp.where(for_even, listed_even, listed_odd)
    blocks = page_table[even // CF * NC + listed]
    return (blocks, row_half, for_even)


def local(
    span_queries,
    span_keys,
    span_values,
    cache_keys,
    cache_values,
    page_table,
    frame_lists,
    list_counts,
    out_weight,
):
    frames = lax.axis_size(FRAME_AXES)
    own_frame = lax.axis_index(FRAME_AXES)
    tokens_here = span_queries.shape[1]
    row_width = span_queries.shape[2]
    heads_here = row_width // HD
    blocks_total, rows_here, _ = cache_keys.shape
    half_rows = rows_here // 2
    half_slots = frame_lists.shape[1] + 1
    own_queries = span_queries[0].reshape(tokens_here, heads_here, HD)
    own_keys = span_keys[0].reshape(tokens_here, heads_here, HD)
    own_values = span_values[0].reshape(tokens_here, heads_here, HD)
    blocks, row_half, for_even = pair_schedule(
        frames, half_slots, page_table, frame_lists, list_counts
    )
    split_keys = cache_keys.reshape(blocks_total, 2, half_rows, row_width)
    split_values = cache_values.reshape(blocks_total, 2, half_rows, row_width)
    sent = jnp.stack([split_keys[blocks, row_half], split_values[blocks, row_half]], axis=1)
    sent = sent.reshape(frames, -1, 128)
    arrived = lax.all_to_all(sent, FRAME_AXES, split_axis=0, concat_axis=0, tiled=True)
    arrived = arrived.reshape(frames, 2, half_slots, half_rows, heads_here, HD)
    arrived = arrived.transpose(1, 2, 0, 3, 4, 5).reshape(
        2, half_slots, frames * half_rows, heads_here, HD
    )
    arrived_keys = arrived[0]
    arrived_values = arrived[1]
    swap = [(i, i ^ 1) for i in range(lax.axis_size("x"))]
    partner_queries = lax.ppermute(own_queries, "x", swap)
    is_even = own_frame % 2 == 0
    mine = for_even[own_frame] == is_even
    own_state = absorb(empty_state(tokens_here, heads_here), own_queries, own_keys, own_values)
    other_state = empty_state(tokens_here, heads_here)

    def advance(slot, states):
        key_block = arrived_keys[slot]
        value_block = arrived_values[slot]

        def take_own(states):
            return (absorb(states[0], own_queries, key_block, value_block), states[1])

        def take_other(states):
            return (states[0], absorb(states[1], partner_queries, key_block, value_block))

        return lax.cond(mine[slot], take_own, take_other, states)

    own_state, other_state = lax.fori_loop(0, half_slots, advance, (own_state, other_state))
    got_max, got_sum, got_out = lax.ppermute(other_state, "x", swap)
    own_max, own_sum, own_out = own_state
    top = jnp.maximum(own_max, got_max)
    own_scale = jnp.exp(own_max - top)
    got_scale = jnp.exp(got_max - top)
    total_sum = own_sum * own_scale + got_sum * got_scale
    total_out = own_out * own_scale[:, :, None] + got_out * got_scale[:, :, None]
    attended = (
        (total_out / total_sum[:, :, None]).astype(jnp.bfloat16).reshape(tokens_here, row_width)
    )
    weight = out_weight
    for axis in reversed(FRAME_AXES):
        weight = lax.all_gather(weight, axis, axis=1, tiled=True)
    partial_value = jnp.dot(attended, weight, preferred_element_type=jnp.float32)
    own_rows = lax.psum_scatter(
        partial_value.astype(jnp.bfloat16), "clip", scatter_dimension=0, tiled=True
    )
    return own_rows[None]


def solution(mesh):
    frames = mesh.shape["fsdp"]
    fine = Mesh(
        np.asarray(mesh.devices).reshape(mesh.shape["clip"], frames // 16, 4, 4),
        ("clip",) + FRAME_AXES,
    )
    in_specs = (
        P(FRAME_AXES, None, "clip"),
        P(FRAME_AXES, None, "clip"),
        P(FRAME_AXES, None, "clip"),
        P(None, FRAME_AXES, "clip"),
        P(None, FRAME_AXES, "clip"),
        P(),
        P(),
        P(),
        P("clip", FRAME_AXES),
    )
    out_specs = P(FRAME_AXES, "clip", None)
    return jax.shard_map(local, mesh=fine, in_specs=in_specs, out_specs=out_specs, check_vma=False)
```

profile of v0, /device:TPU:1, one launch (start us, length us, event | category | flops | bytes accessed | tf_op | source)
XLA Modules:
  0.0 378.0 jit_solution(15196628837934634941)
XLA Ops:
  6.5 13.0 %all_gather.9 = bf16[640,320]{0,1:T(8,128)(2,1)} all-gather(bf16[640,80]{0,1:T(8,128)(2,1)} %param.21), channel_id=1, replica_groups=mesh['clip'=4,'y'=4,'zl'=4,'x'=4] {'x'}, dimensions={1}, use_global_device_ids=true | all-gather | bytes 512000 | tf_op jit(solution)/shard_map/all_gather | solution.py:126
  19.6 2.6 reshape.464
  23.3 2.3 gather_fusion.1
  25.9 2.3 gather_fusion.2
  28.8 3.0 gather_fusion.3
  32.2 2.6 reshape.463
  34.8 7.0 %gather_fusion.5 = bf16[448,4,640]{2,1,0:T(4,128)(2,1)} fusion(bf16[128,2,4,640]{3,2,1,0:T(4,128)(2,1)S(1)} %reshape.464, s32[448]{0:T(512)S(1)} %reshape.497), kind=kCustom, calls=%fused_computation.5 | custom fusion | bytes 4591104 | tf_op jit(solution)/shard_map/gather | solution.py:85
  41.8 7.1 %gather_fusion.4 = bf16[448,4,640]{2,1,0:T(4,128)(2,1)} fusion(bf16[128,2,4,640]{3,2,1,0:T(4,128)(2,1)S(1)} %reshape.463, s32[448]{0:T(512)S(1)} %reshape.497), kind=kCustom, calls=%fused_computation.4 | custom fusion | bytes 4591104 | tf_op jit(solution)/shard_map/gather | solution.py:85
  48.9 7.4 %pad_maximum_fusion = bf16[64,2,7,4,640]{4,3,2,1,0:T(4,128)(2,1)} fusion(bf16[64,1,7,4,640]{4,3,2,1,0:T(4,128)(2,1)} %bitcast.90, bf16[64,1,7,4,640]{4,3,2,1,0:T(4,128)(2,1)} %bitcast.91), kind=kLoop, calls=%fused_computation.39 | loop fusion | flops 2293760 | bytes 9175040 | tf_op jit(solution)/shard_map/stack | solution.py:85
  56.3 8.6 %reshape.465 = bf16[64,280,128]{2,1,0:T(8,128)(2,1)} reshape(bf16[64,2,7,4,640]{4,3,2,1,0:T(4,128)(2,1)} %pad_maximum_fusion) | data formatting | bytes 9175040 | tf_op jit(solution)/shard_map/reshape | solution.py:86
  65.0 10.6 %all-to-all-start = ((bf16[64,280,128]{2,1,0:T(8,128)(2,1)}), bf16[64,280,128]{2,1,0:T(8,128)(2,1)}, u32[]{:S(2)}, u32[]{:S(2)}) async-start(bf16[64,280,128]{2,1,0:T(8,128)(2,1)} %reshape.465), calls=%async_computation | async-start | bytes 9175040 | tf_op jit(solution)/shard_map/all_to_all | solution.py:87
  80.1 2.5 fusion.28
  82.6 1.4 copy.57
  84.0 2.1 copy.55
  87.6 40.7 %collective-permute-done = bf16[512,5,128]{0,2,1:T(8,128)(2,1)} collective-permute-done((bf16[512,5,128]{0,2,1:T(8,128)(2,1)S(1)}, bf16[512,5,128]{0,2,1:T(8,128)(2,1)}, u32[]{:S(2)}, u32[]{:S(2)}) %collective-permute-start) | collective-permute-done | bytes 655392 | tf_op jit(solution)/shard_map/ppermute | solution.py:95
  128.3 2.2 copy.56
  130.5 45.2 %all-to-all-done = bf16[64,280,128]{2,1,0:T(8,128)(2,1)} async-done(((bf16[64,280,128]{2,1,0:T(8,128)(2,1)}), bf16[64,280,128]{2,1,0:T(8,128)(2,1)}, u32[]{:S(2)}, u32[]{:S(2)}) %all-to-all-start) | async-done | bytes 4587552 | tf_op jit(solution)/shard_map/all_to_all | solution.py:87
  175.6 3.5 copy.52
  180.2 3.6 copy.53
  183.8 3.6 copy.54
  187.5 45.5 %while.23 = (s32[]{:T(128)}, f32[512,5]{0,1:T(8,128)S(1)}, f32[512,5]{0,1:T(8,128)S(1)}, f32[512,5,128]{2,1,0:T(8,128)S(1)}, f32[512,5]{0,1:T(8,128)S(1)}, /*ind...) while((s32[]{:T(128)}, f32[512,5]{0,1:T(8,128)S(1)}, ...), condition=%wide.region_9.10_spmd, body=%wide.region_2.9_spmd.sunk | while | flops 341447680 | bytes 15933780 | solution.py:113
  188.7 1.1 dynamic-slice_bitcast_fusion.3
  189.8 4.2 %conditional.2 = (f32[512,5]{0,1:T(8,128)S(1)}, f32[512,5]{0,1:T(8,128)S(1)}, f32[512,5,128]{2,1,0:T(8,128)S(1)}, f32[512,5]{0,1:T(8,128)S(1)}, f32[512,5]{0,1:T(8,128)S(1)}, /*index=5*/f32[512,5,128]{2,0,1:T(8,128)S(1)}) conditional(s32[]{:T(128)} %bitcast.88, (bf16[256,5,128]{2,0,1:T(8,128)(2,1)S(1)}, bf16[512,5,128]{2,0,1:T(8,128)(2,1)}, ...), branch_computations={%region_3.5_spmd, %region_6.8_spmd} | conditional | flops 341447680 | bytes 14602288 | solution.py:111
  189.9 1.8 bitcast_reduce_fusion.1
  195.3 1.1 dynamic-slice_bitcast_fusion.3
  196.5 4.2 %conditional.2 = (f32[512,5]{0,1:T(8,128)S(1)}, f32[512,5]{0,1:T(8,128)S(1)}, f32[512,5,128]{2,1,0:T(8,128)S(1)}, f32[512,5]{0,1:T(8,128)S(1)}, f32[512,5]{0,1:T(8,128)S(1)}, /*index=5*/f32[512,5,128]{2,0,1:T(8,128)S(1)}) conditional(s32[]{:T(128)} %bitcast.88, (bf16[256,5,128]{2,0,1:T(8,128)(2,1)S(1)}, bf16[512,5,128]{2,0,1:T(8,128)(2,1)}, ...), branch_computations={%region_3.5_spmd, %region_6.8_spmd} | conditional | flops 341447680 | bytes 14602288 | solution.py:111
  196.5 1.8 bitcast_reduce_fusion.1
  203.1 4.2 %conditional.2 = (f32[512,5]{0,1:T(8,128)S(1)}, f32[512,5]{0,1:T(8,128)S(1)}, f32[512,5,128]{2,1,0:T(8,128)S(1)}, f32[512,5]{0,1:T(8,128)S(1)}, f32[512,5]{0,1:T(8,128)S(1)}, /*index=5*/f32[512,5,128]{2,0,1:T(8,128)S(1)}) conditional(s32[]{:T(128)} %bitcast.88, (bf16[256,5,128]{2,0,1:T(8,128)(2,1)S(1)}, bf16[512,5,128]{2,0,1:T(8,128)(2,1)}, ...), branch_computations={%region_3.5_spmd, %region_6.8_spmd} | conditional | flops 341447680 | bytes 14602288 | solution.py:111
  203.1 1.7 bitcast_reduce_fusion.1
  208.6 1.1 dynamic-slice_bitcast_fusion.3
  209.7 4.2 %conditional.2 = (f32[512,5]{0,1:T(8,128)S(1)}, f32[512,5]{0,1:T(8,128)S(1)}, f32[512,5,128]{2,1,0:T(8,128)S(1)}, f32[512,5]{0,1:T(8,128)S(1)}, f32[512,5]{0,1:T(8,128)S(1)}, /*index=5*/f32[512,5,128]{2,0,1:T(8,128)S(1)}) conditional(s32[]{:T(128)} %bitcast.88, (bf16[256,5,128]{2,0,1:T(8,128)(2,1)S(1)}, bf16[512,5,128]{2,0,1:T(8,128)(2,1)}, ...), branch_computations={%region_3.5_spmd, %region_6.8_spmd} | conditional | flops 341447680 | bytes 14602288 | solution.py:111
  209.7 1.7 bitcast_reduce_fusion.1
  215.2 1.1 dynamic-slice_bitcast_fusion.3
  216.3 4.2 %conditional.2 = (f32[512,5]{0,1:T(8,128)S(1)}, f32[512,5]{0,1:T(8,128)S(1)}, f32[512,5,128]{2,1,0:T(8,128)S(1)}, f32[512,5]{0,1:T(8,128)S(1)}, f32[512,5]{0,1:T(8,128)S(1)}, /*index=5*/f32[512,5,128]{2,0,1:T(8,128)S(1)}) conditional(s32[]{:T(128)} %bitcast.88, (bf16[256,5,128]{2,0,1:T(8,128)(2,1)S(1)}, bf16[512,5,128]{2,0,1:T(8,128)(2,1)}, ...), branch_computations={%region_3.5_spmd, %region_6.8_spmd} | conditional | flops 341447680 | bytes 14602288 | solution.py:111
  216.3 1.8 bitcast_reduce_fusion.1
  221.8 1.1 dynamic-slice_bitcast_fusion.3
  222.9 4.2 %conditional.2 = (f32[512,5]{0,1:T(8,128)S(1)}, f32[512,5]{0,1:T(8,128)S(1)}, f32[512,5,128]{2,1,0:T(8,128)S(1)}, f32[512,5]{0,1:T(8,128)S(1)}, f32[512,5]{0,1:T(8,128)S(1)}, /*index=5*/f32[512,5,128]{2,0,1:T(8,128)S(1)}) conditional(s32[]{:T(128)} %bitcast.88, (bf16[256,5,128]{2,0,1:T(8,128)(2,1)S(1)}, bf16[512,5,128]{2,0,1:T(8,128)(2,1)}, ...), branch_computations={%region_3.5_spmd, %region_6.8_spmd} | conditional | flops 341447680 | bytes 14602288 | solution.py:111
  223.0 1.8 bitcast_reduce_fusion.1
  228.4 1.1 dynamic-slice_bitcast_fusion.3
  229.5 3.2 conditional.2
  229.6 1.6 bitcast_reduce_fusion
  233.0 1.5 copy.59
  234.5 2.2 collective-permute-start.2
  236.7 1.4 collective-permute-start.1
  238.8 23.3 %collective-permute-done.3 = f32[512,5]{0,1:T(8,128)S(1)} collective-permute-done((f32[512,5]{0,1:T(8,128)S(1)}, f32[512,5]{0,1:T(8,128)S(1)}, u32[]{:S(2)}, u32[]{:S(2)}) %collective-permute-start.3) | collective-permute-done | bytes 10272 | tf_op jit(solution)/shard_map/ppermute | solution.py:114
  262.5 1.7 divide_convert_fusion
  264.2 8.9 %convolution_convert_fusion = bf16[512,5120]{1,0:T(8,128)(2,1)} fusion(bf16[512,640]{0,1:T(8,128)(2,1)S(1)} %bitcast.99, bf16[640,5120]{0,1:T(8,128)(2,1)} %all-gather.5.cloned.1.call-done), kind=kOutput, calls=%fused_computation.35 | convolution fusion | flops 3358064640 | bytes 12451840 | tf_op jit(solution)/shard_map/dot_general | solution.py:127
  273.2 98.3 %reduce-scatter.2.cloned.1.call-done = bf16[128,5120]{1,0:T(8,128)(2,1)} async-done(((bf16[512,5120]{1,0:T(8,128)(2,1)}), bf16[128,5120]{1,0:T(8,128)(2,1)}) %reduce-scatter.2.cloned.1.call-update) | async-done | bytes 1310736 | tf_op jit(solution)/shard_map/reduce_scatter | solution.py:128
  (120 shorter events, 31.7 us)
Async XLA Ops:
  6.5 16.8 %copy-start = (s32[64,6]{0,1:T(8,128)S(1)}, s32[64,6]{0,1:T(8,128)}, u32[]{:S(2)}) copy-start(s32[64,6]{0,1:T(8,128)} %param.19) | copy-start | bytes 4612
  6.5 15.7 %copy-start.3 = (s32[64]{0:T(128)S(1)}, s32[64]{0:T(128)}, u32[]{:S(2)}) copy-start(s32[64]{0:T(128)} %param.20) | copy-start | bytes 772
  6.5 69.1 %all-gather.3.cloned.1.call-start = ((), (), s32[]{:S(2)}) async-start(), calls=%async_computation.2 | async-start | bytes 2048000 | tf_op jit(solution)/shard_map/all_gather | solution.py:126
  28.2 0.7 copy-start.2
  65.0 11.4 %copy-start.4 = (bf16[1,512,640]{2,1,0:T(8,128)(2,1)S(1)}, bf16[1,512,640]{2,1,0:T(8,128)(2,1)}, u32[]{:S(2)}) copy-start(bf16[1,512,640]{2,1,0:T(8,128)(2,1)} %param.13) | copy-start | bytes 1966084
  65.0 110.6 %all-to-all-start = ((bf16[64,280,128]{2,1,0:T(8,128)(2,1)}), bf16[64,280,128]{2,1,0:T(8,128)(2,1)}, u32[]{:S(2)}, u32[]{:S(2)}) async-start(bf16[64,280,128]{2,1,0:T(8,128)(2,1)} %reshape.465), calls=%async_computation | async-start | bytes 9175040 | tf_op jit(solution)/shard_map/all_to_all | solution.py:87
  75.6 2.1 copy-start.5
  75.6 2.4 copy-start.6
  75.6 188.6 %all-gather.5.cloned.1.call-start = ((), (), s32[]{:S(2)}) async-start(), calls=%async_computation.3 | async-start | bytes 8192000 | tf_op jit(solution)/shard_map/all_gather | solution.py:126
  76.4 295.1 %reduce-scatter.2.cloned.1.call-start = ((), (), s32[]{:S(2)}) async-start(), calls=%async_computation.4 | async-start | bytes 6553600 | tf_op jit(solution)/shard_map/reduce_scatter | solution.py:128
  76.7 51.6 %collective-permute-start = (bf16[512,5,128]{0,2,1:T(8,128)(2,1)S(1)}, bf16[512,5,128]{0,2,1:T(8,128)(2,1)}, u32[]{:S(2)}, u32[]{:S(2)}) collective-permute-start(bf16[512,5,128]{0,2,1:T(8,128)(2,1)S(1)} %bitcast.94), channel_id=1, source_target_pairs={{0,1},{1,0},{2,3},{3,2},{4,5},{5,4},{6,7},{7,6},{8,9},{9,8},{10,11... | collective-permute-start | bytes 1966088 | tf_op jit(solution)/shard_map/ppermute | solution.py:95
  234.5 28.0 %collective-permute-start.2 = (f32[512,5,128]{0,2,1:T(8,128)}, f32[512,5,128]{0,2,1:T(8,128)}, u32[]{:S(2)}, u32[]{:S(2)}) collective-permute-start(f32[512,5,128]{0,2,1:T(8,128)} %copy.59), channel_id=1, source_target_pairs={{0,1},{1,0},{2,3},{3,2},{4,5},{5,4},{6,7},{7,6},{8,9},{9,8},{10,11... | collective-permute-start | bytes 3932168 | tf_op jit(solution)/shard_map/ppermute | solution.py:114
  236.7 25.4 %collective-permute-start.3 = (f32[512,5]{0,1:T(8,128)S(1)}, f32[512,5]{0,1:T(8,128)S(1)}, u32[]{:S(2)}, u32[]{:S(2)}) collective-permute-start(f32[512,5]{0,1:T(8,128)S(1)} %get-tuple-element.286), channel_id=1, source_target_pairs={{0,1},{1,0},{2,3},{3,2},{4,5},{5,4},{6,7},{7,6},{8,9},{9,8},{10,11... | collective-permute-start | bytes 30728 | tf_op jit(solution)/shard_map/ppermute | solution.py:114
  236.7 25.7 %collective-permute-start.1 = (f32[512,5]{0,1:T(8,128)S(1)}, f32[512,5]{0,1:T(8,128)S(1)}, u32[]{:S(2)}, u32[]{:S(2)}) collective-permute-start(f32[512,5]{0,1:T(8,128)S(1)} %get-tuple-element.283), channel_id=1, source_target_pairs={{0,1},{1,0},{2,3},{3,2},{4,5},{5,4},{6,7},{7,6},{8,9},{9,8},{10,11... | collective-permute-start | bytes 30728 | tf_op jit(solution)/shard_map/ppermute | solution.py:114
  273.1 98.3 %copy-start.1 = (s32[64,6]{0,1:T(8,128)S(1)}, s32[64,6]{0,1:T(8,128)}, u32[]{:S(2)}) copy-start(s32[64,6]{0,1:T(8,128)} %param.19) | copy-start | bytes 4612
Sparse Core Ops, SparseCore 0:
  19.7 46.3 all-gather.2
  78.2 106.0 all-gather.4
  273.3 98.1 reduce-scatter.1
where the time goes:
time: 379 us; the launch traced here: 378 us
  waiting for transfers between devices  209 us (55%)
  local copies, waits for them, and re-layouts  75.5 us (20%)
  matrix products  32.2 us (8%)
  starting transfers between devices  15.4 us (4%)
  other arithmetic  14.5 us (4%)
  between operations  13.4 us (4%)
  blocking collectives  13 us (3%)
  loops' own time  5.42 us (1%)
    reduce_scatter x1, waiting for transfers between devices, local(): lax.psum_scatter(partial_value.astype(jnp.bfloat16), 'clip', scatter_dime...  98.3 us
    all_to_all x1, waiting for transfers between devices, local(): lax.all_to_all(sent, FRAME_AXES, split_axis=0, concat_axis=0, tiled=True)  45.2 us
    ppermute x1, waiting for transfers between devices, local(): partner_queries = lax.ppermute(own_queries, 'x', swap)  40.7 us
    ppermute x3, waiting for transfers between devices, local(): got_max, got_sum, got_out = lax.ppermute(other_state, 'x', swap)  23.6 us
    dot_general x8, matrix products, absorb(): jnp.einsum('qhd,khd->qhk', query_block, key_block, preferred_element_type...  13 us
    all_gather x1, blocking collectives, local(): weight = lax.all_gather(weight, axis, axis=1, tiled=True)  13 us
    all_to_all x1, starting transfers between devices, local(): lax.all_to_all(sent, FRAME_AXES, split_axis=0, concat_axis=0, tiled=True)  10.6 us
    dot_general x8, matrix products, absorb(): jnp.einsum('qhk,khd->qhd', weights.astype(jnp.bfloat16), value_block, pre...  10.3 us
  transfers between devices with their start and end apart: 8, of which 5 were waited for; matrix products, arithmetic and copies ran while one was open for 30% of the time, Pallas kernels for 0%

commit v1 on v0

--- a/solution.py
+++ b/solution.py
@@ -123,7 +123,9 @@
     )
     weight = out_weight
     for axis in reversed(FRAME_AXES):
-        weight = lax.all_gather(weight, axis, axis=1, tiled=True)
+        weight = jnp.concatenate(
+            lax.all_to_all(jnp.stack([weight] * lax.axis_size(axis)), axis, 0, 0), axis=1
+        )
     partial_value = jnp.dot(attended, weight, preferred_element_type=jnp.float32)
     own_rows = lax.psum_scatter(
         partial_value.astype(jnp.bfloat16), "clip", scatter_dimension=0, tiled=True

time: 379 us -> 414 us (1.092)
  waiting for transfers between devices: 209 us -> 225 us
  starting transfers between devices: 15.4 us -> 24.4 us
  local copies, waits for them, and re-layouts: 75.5 us -> 80.8 us
    all_to_all x1, waiting for transfers between devices: 45.2 us -> 99.8 us  [local(): lax.all_to_all(sent, FRAME_AXES, split_axis=0, concat_axis=0, tiled=True)]
    ppermute x1, waiting for transfers between devices: 40.7 us -> 0.01 us  [local(): partner_queries = lax.ppermute(own_queries, 'x', swap)]
    all_gather x1 -> x0, blocking collectives: 13 us -> none  [local(): weight = lax.all_gather(weight, axis, axis=1, tiled=True)]
    all_to_all x0 -> x1, blocking collectives: none -> 11.9 us  [local(): lax.all_to_all(jnp.stack([weight] * lax.axis_size(axis)), axis, 0, 0)]
    all_to_all x0 -> x2, starting transfers between devices: none -> 11 us  [local(): lax.all_to_all(jnp.stack([weight] * lax.axis_size(axis)), axis, 0, 0)]
    another operation x9 -> x12, local copies, waits for them, and re-layouts: 4.97 us -> 11.9 us  [the longest x3 6.96 us: local(): jnp.stack([weight] * lax.axis_size(axis))]
  transfers between devices with their start and end apart: 8 -> 8, of which waited for: 5 -> 4; matrix products, arithmetic and copies ran while one was open for 30% -> 29% of each run, Pallas kernels for 0% -> 0%
where the time goes in v1:
time: 414 us; the launch traced here: 413 us
  waiting for transfers between devices  225 us (54%)
  local copies, waits for them, and re-layouts  80.8 us (20%)
  matrix products  34.5 us (8%)
  starting transfers between devices  24.4 us (6%)
  other arithmetic  17.1 us (4%)
  between operations  13.7 us (3%)
  blocking collectives  11.9 us (3%)
  loops' own time  5.83 us (1%)
    reduce_scatter x1, waiting for transfers between devices, local(): lax.psum_scatter(partial_value.astype(jnp.bfloat16), 'clip', scatter_dime...  101 us
    all_to_all x1, waiting for transfers between devices, local(): lax.all_to_all(sent, FRAME_AXES, split_axis=0, concat_axis=0, tiled=True)  99.8 us
    ppermute x3, waiting for transfers between devices, local(): got_max, got_sum, got_out = lax.ppermute(other_state, 'x', swap)  23.8 us
    dot_general x8, matrix products, absorb(): jnp.einsum('qhd,khd->qhk', query_block, key_block, preferred_element_type...  15.3 us
    all_to_all x1, blocking collectives, local(): lax.all_to_all(jnp.stack([weight] * lax.axis_size(axis)), axis, 0, 0)  11.9 us
    all_to_all x2, starting transfers between devices, local(): lax.all_to_all(jnp.stack([weight] * lax.axis_size(axis)), axis, 0, 0)  11 us
    dot_general x8, matrix products, absorb(): jnp.einsum('qhk,khd->qhd', weights.astype(jnp.bfloat16), value_block, pre...  10.3 us
    all_to_all x1, starting transfers between devices, local(): lax.all_to_all(sent, FRAME_AXES, split_axis=0, concat_axis=0, tiled=True)  9.41 us
  transfers between devices with their start and end apart: 8, of which 4 were waited for; matrix products, arithmetic and copies ran while one was open for 29% of the time, Pallas kernels for 0%

profile of v1, /device:TPU:1, one launch (start us, length us, event | category | flops | bytes accessed | tf_op | source)
XLA Modules:
  0.0 412.9 jit_solution(1879173500305536432)
XLA Ops:
  7.5 11.9 %all_to_all.20 = bf16[4,640,80]{1,2,0:T(8,128)(2,1)S(1)} all-to-all(bf16[4,640,80]{1,2,0:T(8,128)(2,1)S(1)} %stack.25), channel_id=1, replica_groups=mesh['clip'=4,'y'=4,'zl'=4,'x'=4] {'x'}, dimensions={0} | all-to-all | bytes 819200 | tf_op jit(solution)/shard_map/all_to_all | solution.py:127
  19.3 1.3 stack.26
  20.7 5.7 %all-to-all-start.2 = ((bf16[4,640,320]{1,2,0:T(8,128)(2,1)}), bf16[4,640,320]{1,2,0:T(8,128)(2,1)}, u32[]{:S(2)}, u32[]{:S(2)}) async-start(bf16[4,640,320]{1,2,0:T(8,128)(2,1)} %stack.26), calls=%async_computation.2 | async-start | bytes 3276800 | tf_op jit(solution)/shard_map/all_to_all | solution.py:127
  27.9 2.3 gather_fusion.1
  30.4 2.3 gather_fusion.2
  33.4 3.0 gather_fusion.3
  36.8 2.6 reshape.481
  39.4 7.0 %gather_fusion.5 = bf16[448,4,640]{2,1,0:T(4,128)(2,1)} fusion(bf16[128,2,4,640]{3,2,1,0:T(4,128)(2,1)S(1)} %reshape.482, s32[448]{0:T(512)S(1)} %reshape.519), kind=kCustom, calls=%fused_computation.5 | custom fusion | bytes 4591104 | tf_op jit(solution)/shard_map/gather | solution.py:85
  46.4 7.0 %gather_fusion.4 = bf16[448,4,640]{2,1,0:T(4,128)(2,1)} fusion(bf16[128,2,4,640]{3,2,1,0:T(4,128)(2,1)S(1)} %reshape.481, s32[448]{0:T(512)S(1)} %reshape.519), kind=kCustom, calls=%fused_computation.4 | custom fusion | bytes 4591104 | tf_op jit(solution)/shard_map/gather | solution.py:85
  53.3 7.4 %pad_maximum_fusion = bf16[64,2,7,4,640]{4,3,2,1,0:T(4,128)(2,1)} fusion(bf16[64,1,7,4,640]{4,3,2,1,0:T(4,128)(2,1)} %bitcast.99, bf16[64,1,7,4,640]{4,3,2,1,0:T(4,128)(2,1)} %bitcast.100), kind=kLoop, calls=%fused_computation.39 | loop fusion | flops 2293760 | bytes 9175040 | tf_op jit(solution)/shard_map/stack | solution.py:85
  60.8 8.6 %reshape.483 = bf16[64,280,128]{2,1,0:T(8,128)(2,1)} reshape(bf16[64,2,7,4,640]{4,3,2,1,0:T(4,128)(2,1)} %pad_maximum_fusion) | data formatting | bytes 9175040 | tf_op jit(solution)/shard_map/reshape | solution.py:86
  69.4 9.4 %all-to-all-start = ((bf16[64,280,128]{2,1,0:T(8,128)(2,1)}), bf16[64,280,128]{2,1,0:T(8,128)(2,1)}, u32[]{:S(2)}, u32[]{:S(2)}) async-start(bf16[64,280,128]{2,1,0:T(8,128)(2,1)} %reshape.483), calls=%async_computation | async-start | bytes 9175040 | tf_op jit(solution)/shard_map/all_to_all | solution.py:87
  80.4 99.8 %all-to-all-done = bf16[64,280,128]{2,1,0:T(8,128)(2,1)} async-done(((bf16[64,280,128]{2,1,0:T(8,128)(2,1)}), bf16[64,280,128]{2,1,0:T(8,128)(2,1)}, u32[]{:S(2)}, u32[]{:S(2)}) %all-to-all-start) | async-done | bytes 4587552 | tf_op jit(solution)/shard_map/all_to_all | solution.py:87
  180.3 4.7 %stack.27 = bf16[4,640,1280]{1,2,0:T(8,128)(2,1)} broadcast(bf16[640,1280]{0,1:T(8,128)(2,1)} %bitcast.25), dimensions={1,2} | broadcast | bytes 8192000 | tf_op jit(solution)/shard_map/stack | solution.py:127
  185.0 5.3 %all-to-all-start.3 = ((bf16[4,640,1280]{1,2,0:T(8,128)(2,1)}), bf16[4,640,1280]{1,2,0:T(8,128)(2,1)}, u32[]{:S(2)}, u32[]{:S(2)}) async-start(bf16[4,640,1280]{1,2,0:T(8,128)(2,1)} %stack.27), calls=%async_computation.3 | async-start | bytes 13107200 | tf_op jit(solution)/shard_map/all_to_all | solution.py:127
  190.3 3.2 bitcast_reduce_fusion.2
  193.8 3.5 fusion.20
  197.8 2.5 fusion.28
  200.3 1.4 copy.58
  201.8 2.1 copy.56
  205.3 2.2 copy.57
  207.5 3.5 copy.53
  212.1 3.5 copy.54
  215.6 3.5 copy.55
  219.2 46.4 %while.23 = (s32[]{:T(128)}, f32[512,5]{0,1:T(8,128)S(1)}, f32[512,5]{0,1:T(8,128)S(1)}, f32[512,5,128]{2,1,0:T(8,128)S(1)}, f32[512,5]{0,1:T(8,128)S(1)}, /*ind...) while((s32[]{:T(128)}, f32[512,5]{0,1:T(8,128)S(1)}, ...), condition=%wide.region_9.10_spmd, body=%wide.region_2.9_spmd.sunk | while | flops 341447680 | bytes 15933780 | solution.py:113
  221.7 4.2 %conditional.2 = (f32[512,5]{0,1:T(8,128)S(1)}, f32[512,5]{0,1:T(8,128)S(1)}, f32[512,5,128]{2,1,0:T(8,128)S(1)}, f32[512,5]{0,1:T(8,128)S(1)}, f32[512,5]{0,1:T(8,128)S(1)}, /*index=5*/f32[512,5,128]{2,0,1:T(8,128)S(1)}) conditional(s32[]{:T(128)} %bitcast.97, (bf16[256,5,128]{2,0,1:T(8,128)(2,1)S(1)}, bf16[512,5,128]{2,0,1:T(8,128)(2,1)}, ...), branch_computations={%region_3.5_spmd, %region_6.8_spmd} | conditional | flops 341447680 | bytes 14602288 | solution.py:111
  221.7 1.7 bitcast_reduce_fusion.1
  227.3 1.1 dynamic-slice_bitcast_fusion.3
  228.5 4.2 %conditional.2 = (f32[512,5]{0,1:T(8,128)S(1)}, f32[512,5]{0,1:T(8,128)S(1)}, f32[512,5,128]{2,1,0:T(8,128)S(1)}, f32[512,5]{0,1:T(8,128)S(1)}, f32[512,5]{0,1:T(8,128)S(1)}, /*index=5*/f32[512,5,128]{2,0,1:T(8,128)S(1)}) conditional(s32[]{:T(128)} %bitcast.97, (bf16[256,5,128]{2,0,1:T(8,128)(2,1)S(1)}, bf16[512,5,128]{2,0,1:T(8,128)(2,1)}, ...), branch_computations={%region_3.5_spmd, %region_6.8_spmd} | conditional | flops 341447680 | bytes 14602288 | solution.py:111
  228.5 1.8 bitcast_reduce_fusion.1
  234.1 1.1 dynamic-slice_bitcast_fusion.3
  235.2 4.2 %conditional.2 = (f32[512,5]{0,1:T(8,128)S(1)}, f32[512,5]{0,1:T(8,128)S(1)}, f32[512,5,128]{2,1,0:T(8,128)S(1)}, f32[512,5]{0,1:T(8,128)S(1)}, f32[512,5]{0,1:T(8,128)S(1)}, /*index=5*/f32[512,5,128]{2,0,1:T(8,128)S(1)}) conditional(s32[]{:T(128)} %bitcast.97, (bf16[256,5,128]{2,0,1:T(8,128)(2,1)S(1)}, bf16[512,5,128]{2,0,1:T(8,128)(2,1)}, ...), branch_computations={%region_3.5_spmd, %region_6.8_spmd} | conditional | flops 341447680 | bytes 14602288 | solution.py:111
  235.2 1.7 bitcast_reduce_fusion.1
  241.9 4.2 %conditional.2 = (f32[512,5]{0,1:T(8,128)S(1)}, f32[512,5]{0,1:T(8,128)S(1)}, f32[512,5,128]{2,1,0:T(8,128)S(1)}, f32[512,5]{0,1:T(8,128)S(1)}, f32[512,5]{0,1:T(8,128)S(1)}, /*index=5*/f32[512,5,128]{2,0,1:T(8,128)S(1)}) conditional(s32[]{:T(128)} %bitcast.97, (bf16[256,5,128]{2,0,1:T(8,128)(2,1)S(1)}, bf16[512,5,128]{2,0,1:T(8,128)(2,1)}, ...), branch_computations={%region_3.5_spmd, %region_6.8_spmd} | conditional | flops 341447680 | bytes 14602288 | solution.py:111
  242.0 1.8 bitcast_reduce_fusion.1
  248.7 4.2 %conditional.2 = (f32[512,5]{0,1:T(8,128)S(1)}, f32[512,5]{0,1:T(8,128)S(1)}, f32[512,5,128]{2,1,0:T(8,128)S(1)}, f32[512,5]{0,1:T(8,128)S(1)}, f32[512,5]{0,1:T(8,128)S(1)}, /*index=5*/f32[512,5,128]{2,0,1:T(8,128)S(1)}) conditional(s32[]{:T(128)} %bitcast.97, (bf16[256,5,128]{2,0,1:T(8,128)(2,1)S(1)}, bf16[512,5,128]{2,0,1:T(8,128)(2,1)}, ...), branch_computations={%region_3.5_spmd, %region_6.8_spmd} | conditional | flops 341447680 | bytes 14602288 | solution.py:111
  248.7 1.8 bitcast_reduce_fusion.1
  255.4 4.2 %conditional.2 = (f32[512,5]{0,1:T(8,128)S(1)}, f32[512,5]{0,1:T(8,128)S(1)}, f32[512,5,128]{2,1,0:T(8,128)S(1)}, f32[512,5]{0,1:T(8,128)S(1)}, f32[512,5]{0,1:T(8,128)S(1)}, /*index=5*/f32[512,5,128]{2,0,1:T(8,128)S(1)}) conditional(s32[]{:T(128)} %bitcast.97, (bf16[256,5,128]{2,0,1:T(8,128)(2,1)S(1)}, bf16[512,5,128]{2,0,1:T(8,128)(2,1)}, ...), branch_computations={%region_3.5_spmd, %region_6.8_spmd} | conditional | flops 341447680 | bytes 14602288 | solution.py:111
  255.4 1.8 bitcast_reduce_fusion.1
  262.2 3.2 conditional.2
  262.2 1.6 bitcast_reduce_fusion
  265.6 1.5 copy.60
  267.1 1.4 collective-permute-start.2
  268.5 1.4 collective-permute-start.1
  270.6 23.5 %collective-permute-done.3 = f32[512,5]{0,1:T(8,128)S(1)} collective-permute-done((f32[512,5]{0,1:T(8,128)S(1)}, f32[512,5]{0,1:T(8,128)S(1)}, u32[]{:S(2)}, u32[]{:S(2)}) %collective-permute-start.3) | collective-permute-done | bytes 10272 | tf_op jit(solution)/shard_map/ppermute | solution.py:114
  294.4 1.7 divide_convert_fusion
  296.1 9.0 %convolution_convert_fusion = bf16[512,5120]{1,0:T(8,128)(2,1)} fusion(bf16[512,640]{0,1:T(8,128)(2,1)S(1)} %bitcast.109, bf16[640,5120]{0,1:T(8,128)(2,1)} %bitcast.27), kind=kOutput, calls=%fused_computation.35 | convolution fusion | flops 3358064640 | bytes 12451840 | tf_op jit(solution)/shard_map/dot_general | solution.py:129
  305.1 100.9 %reduce-scatter.2.cloned.1.call-done = bf16[128,5120]{1,0:T(8,128)(2,1)} async-done(((bf16[512,5120]{1,0:T(8,128)(2,1)}), bf16[128,5120]{1,0:T(8,128)(2,1)}) %reduce-scatter.2.cloned.1.call-update) | async-done | bytes 1310736 | tf_op jit(solution)/shard_map/reduce_scatter | solution.py:130
  (125 shorter events, 35.9 us)
Async XLA Ops:
  6.5 21.3 %copy-start = (s32[64,6]{0,1:T(8,128)S(1)}, s32[64,6]{0,1:T(8,128)}, u32[]{:S(2)}) copy-start(s32[64,6]{0,1:T(8,128)} %param.19) | copy-start | bytes 4612
  19.3 7.1 %copy-start.5 = (bf16[128,8,640]{2,1,0:T(8,128)(2,1)S(1)}, bf16[128,8,640]{2,1,0:T(8,128)(2,1)}, u32[]{:S(2)}) copy-start(bf16[128,8,640]{2,1,0:T(8,128)(2,1)} %param.17) | copy-start | bytes 3932164
  20.7 6.1 %copy-start.3 = (s32[64]{0:T(128)S(1)}, s32[64]{0:T(128)}, u32[]{:S(2)}) copy-start(s32[64]{0:T(128)} %param.20) | copy-start | bytes 772
  20.7 48.8 %all-to-all-start.2 = ((bf16[4,640,320]{1,2,0:T(8,128)(2,1)}), bf16[4,640,320]{1,2,0:T(8,128)(2,1)}, u32[]{:S(2)}, u32[]{:S(2)}) async-start(bf16[4,640,320]{1,2,0:T(8,128)(2,1)} %stack.26), calls=%async_computation.2 | async-start | bytes 3276800 | tf_op jit(solution)/shard_map/all_to_all | solution.py:127
  32.7 0.7 copy-start.2
  69.4 9.4 %copy-start.6 = (bf16[1,512,640]{2,1,0:T(8,128)(2,1)S(1)}, bf16[1,512,640]{2,1,0:T(8,128)(2,1)}, u32[]{:S(2)}) copy-start(bf16[1,512,640]{2,1,0:T(8,128)(2,1)} %param.13) | copy-start | bytes 1966084
  69.4 10.7 %copy-start.7 = (bf16[1,512,640]{2,1,0:T(8,128)(2,1)S(1)}, bf16[1,512,640]{2,1,0:T(8,128)(2,1)}, u32[]{:S(2)}) copy-start(bf16[1,512,640]{2,1,0:T(8,128)(2,1)} %param.14) | copy-start | bytes 1966084
  69.4 110.8 %all-to-all-start = ((bf16[64,280,128]{2,1,0:T(8,128)(2,1)}), bf16[64,280,128]{2,1,0:T(8,128)(2,1)}, u32[]{:S(2)}, u32[]{:S(2)}) async-start(bf16[64,280,128]{2,1,0:T(8,128)(2,1)} %reshape.483), calls=%async_computation | async-start | bytes 9175040 | tf_op jit(solution)/shard_map/all_to_all | solution.py:87
  79.1 126.2 %collective-permute-start = (bf16[512,5,128]{0,2,1:T(8,128)(2,1)S(1)}, bf16[512,5,128]{0,2,1:T(8,128)(2,1)}, u32[]{:S(2)}, u32[]{:S(2)}) collective-permute-start(bf16[512,5,128]{0,2,1:T(8,128)(2,1)S(1)} %bitcast.103), channel_id=1, source_target_pairs={{0,1},{1,0},{2,3},{3,2},{4,5},{5,4},{6,7},{7,6},{8,9},{9,8},{10,11... | collective-permute-start | bytes 1966088 | tf_op jit(solution)/shard_map/ppermute | solution.py:95
  185.0 111.2 %all-to-all-start.3 = ((bf16[4,640,1280]{1,2,0:T(8,128)(2,1)}), bf16[4,640,1280]{1,2,0:T(8,128)(2,1)}, u32[]{:S(2)}, u32[]{:S(2)}) async-start(bf16[4,640,1280]{1,2,0:T(8,128)(2,1)} %stack.27), calls=%async_computation.3 | async-start | bytes 13107200 | tf_op jit(solution)/shard_map/all_to_all | solution.py:127
  190.3 215.8 %reduce-scatter.2.cloned.1.call-start = ((), (), s32[]{:S(2)}) async-start(), calls=%async_computation.5 | async-start | bytes 6553600 | tf_op jit(solution)/shard_map/reduce_scatter | solution.py:130
  190.3 3.2 copy-start.8
  193.8 4.0 copy-start.4
  267.1 27.3 %collective-permute-start.2 = (f32[512,5,128]{0,2,1:T(8,128)}, f32[512,5,128]{0,2,1:T(8,128)}, u32[]{:S(2)}, u32[]{:S(2)}) collective-permute-start(f32[512,5,128]{0,2,1:T(8,128)} %copy.60), channel_id=1, source_target_pairs={{0,1},{1,0},{2,3},{3,2},{4,5},{5,4},{6,7},{7,6},{8,9},{9,8},{10,11... | collective-permute-start | bytes 3932168 | tf_op jit(solution)/shard_map/ppermute | solution.py:114
  268.4 25.6 %collective-permute-start.3 = (f32[512,5]{0,1:T(8,128)S(1)}, f32[512,5]{0,1:T(8,128)S(1)}, u32[]{:S(2)}, u32[]{:S(2)}) collective-permute-start(f32[512,5]{0,1:T(8,128)S(1)} %get-tuple-element.286), channel_id=1, source_target_pairs={{0,1},{1,0},{2,3},{3,2},{4,5},{5,4},{6,7},{7,6},{8,9},{9,8},{10,11... | collective-permute-start | bytes 30728 | tf_op jit(solution)/shard_map/ppermute | solution.py:114
  268.5 25.9 %collective-permute-start.1 = (f32[512,5]{0,1:T(8,128)S(1)}, f32[512,5]{0,1:T(8,128)S(1)}, u32[]{:S(2)}, u32[]{:S(2)}) collective-permute-start(f32[512,5]{0,1:T(8,128)S(1)} %get-tuple-element.283), channel_id=1, source_target_pairs={{0,1},{1,0},{2,3},{3,2},{4,5},{5,4},{6,7},{7,6},{8,9},{9,8},{10,11... | collective-permute-start | bytes 30728 | tf_op jit(solution)/shard_map/ppermute | solution.py:114
  305.1 101.0 %copy-start.1 = (s32[64,6]{0,1:T(8,128)S(1)}, s32[64,6]{0,1:T(8,128)}, u32[]{:S(2)}) copy-start(s32[64,6]{0,1:T(8,128)} %param.19) | copy-start | bytes 4612
Sparse Core Ops, SparseCore 0:
  305.2 100.7 reduce-scatter.1
